TPU v7x, 32 devices: a whole 2x2x4 slice. The times are simulated.
32 devices in a mesh: outer: 8 (over z, y), inner: 4 (over x, core).
Axes of the slice: x: 2, y: 2, z: 4, core: 2. Of those that a mesh axis runs over, the one named last changes fastest.
Arguments:
- qkv_blocks: bfloat16 [4096, 16, 512], P(('outer', 'inner')), may hold values from -4 to 4
- block_scales: bfloat16 [128, 16, 4], P(('outer', 'inner')), may hold values from 0.25 to 4
- gate_logits: bfloat16 [4096, 16, 4], P(('outer', 'inner')), may hold values from -5 to 45056
- conv_weight: float32 [4, 16, 512], P(None, 'inner'), may hold values from -3 to 3
- decay_log: float32 [32], P('inner'), may hold values from -15 to -3
- dt_bias: float32 [32], P('inner'), may hold values from -1 to 1
- norm_gain: float32 [128], replicated, may hold values from 0.5 to 1.5
Outputs:
- normed_heads: bfloat16 [4096, 32, 128], P(('outer', 'inner'))
All inputs are finite; a program needn't handle non-finite values.
Results may differ from a plain program's by a relative error of at most 0.0004.
Values may be sent and summed in bfloat16 or wider, within the bound.
No kernel may reach another device: no remote copies, remote signals or barrier semaphores. Data moves between devices by JAX's collectives and lax.ppermute only.
A program may use at most 128 MiB of HBM per device.

v0:
```python
import jax
import jax.numpy as jnp
from jax import lax
from jax.sharding import PartitionSpec as P

HD = 128
BLOCK = 128
QB = 32
CONV = 4


HIGH_PRECISION = lax.Precision.HIGHEST
EPS_NORM = 1e-06


def convolve(extended, conv_weight, token_count):
    summed = conv_weight[0] * extended[0:token_count]
    for offset in range(1, CONV):
        summed = summed + conv_weight[offset] * extended[offset : offset + token_count]
    return jax.nn.silu(summed)


def unit_rows(matrix):
    return matrix * lax.rsqrt(jnp.sum(matrix * matrix, axis=-1, keepdims=True) + EPS_NORM)


def split_heads(mixed, gate_share, decay_log, dt_bias):
    token_count = mixed.shape[0]
    value_heads = 2 * mixed.shape[1]
    block_count = token_count // BLOCK
    query_heads = unit_rows(mixed[:, :, :HD])
    key_heads = unit_rows(mixed[:, :, HD : 2 * HD])
    queries = jnp.repeat(query_heads, 2, axis=1)
    keys_in = jnp.repeat(key_heads, 2, axis=1)
    values_in = mixed[:, :, 2 * HD :].reshape(token_count, value_heads, HD)
    gate_values = gate_share.astype(jnp.float32)
    beta_gate = jax.nn.sigmoid(gate_values[:, :, :2].reshape(token_count, value_heads))
    raw_decay = gate_values[:, :, 2:].reshape(token_count, value_heads)
    log_decay = -jnp.exp(decay_log) * jax.nn.softplus(raw_decay + dt_bias)

    def blocked(tensor):
        return jnp.swapaxes(tensor.reshape((block_count, BLOCK) + tensor.shape[1:]), 1, 2)

    return (
        blocked(query_heads),
        blocked(key_heads),
        blocked(queries),
        blocked(keys_in),
        blocked(values_in),
        blocked(beta_gate),
        blocked(log_decay),
    )


def lower_inverse(strict_part, length):
    negated = -strict_part
    eye_block = jnp.eye(length, dtype=jnp.float32)

    def level(unused_level, carried):
        inverse, power = carried
        power = jnp.einsum("...ij,...jk->...ik", power, power, precision=HIGH_PRECISION)
        inverse = inverse + jnp.einsum(
            "...ij,...jk->...ik", inverse, power, precision=HIGH_PRECISION
        )
        return (inverse, power)

    levels = (length - 1).bit_length() - 1
    return lax.fori_loop(0, levels, level, (eye_block + negated, negated))[0]


def block_terms(query_heads, key_heads, queries, keys_in, values_in, beta_gate, log_decay):
    cumulative = jnp.cumsum(log_decay, axis=-1)
    length = log_decay.shape[-1]
    row_index = lax.broadcasted_iota(jnp.int32, (length, length), 0)
    col_index = lax.broadcasted_iota(jnp.int32, (length, length), 1)
    lower_mask = row_index >= col_index
    strict = row_index > col_index
    differ = cumulative[..., :, None] - cumulative[..., None, :]
    weights = jnp.where(lower_mask, jnp.exp(jnp.where(lower_mask, differ, 0.0)), 0.0)
    both = jnp.concatenate([key_heads, query_heads], axis=-2)
    dots = jnp.einsum("...cd,...ed->...ce", both, key_heads, precision=HIGH_PRECISION)
    dots = jnp.repeat(dots, 2, axis=-3)
    key_dots = dots[..., :length, :]
    strict_part = jnp.where(strict, key_dots * weights * beta_gate[..., :, None], 0.0)
    growth = jnp.exp(cumulative)
    right_side = jnp.concatenate(
        [beta_gate[..., None] * values_in, (beta_gate * growth)[..., None] * keys_in], axis=-1
    )
    inverse = lower_inverse(strict_part, length)
    solved = jnp.einsum("...ce,...ed->...cd", inverse, right_side, precision=HIGH_PRECISION)
    attend = dots[..., length:, :] * weights
    final_sum = cumulative[..., -1]
    carried_keys = jnp.exp(final_sum[..., None] - cumulative)[..., None] * keys_in
    return (
        solved,
        attend,
        growth[..., None] * queries,
        carried_keys,
        jnp.exp(final_sum),
    )


def advance(current_state, incoming_value_rows, carried_keys, decay_total):
    return decay_total[..., None, None] * current_state + jnp.einsum(
        "...ck,...cv->...kv", carried_keys, incoming_value_rows, precision=HIGH_PRECISION
    )


def pair_update(passed_block_state, inputs):
    current_update, current_write, carried_now, decay_now = inputs
    target_values = jnp.concatenate([current_update, jnp.zeros_like(current_update)], axis=-1)
    incoming_value_rows = target_values - jnp.einsum(
        "zsg,zgj->zsj", current_write, passed_block_state, precision=HIGH_PRECISION
    )
    return advance(passed_block_state, incoming_value_rows, carried_now, decay_now)


def shifted(value, axis, steps):
    count = lax.axis_size(axis)
    return lax.ppermute(value, axis, [(source, source + steps) for source in range(count - steps)])


def incoming_state(pair, axis):
    count = lax.axis_size(axis)
    place = lax.axis_index(axis)
    state = pair[..., :HD]
    if count == 1:
        return jnp.zeros_like(state)
    width = 1
    while 2 * width < count:
        got = shifted(pair, axis, width)
        joined = jnp.einsum("hij,hjk->hik", pair[..., HD:], got, precision=HIGH_PRECISION)
        joined = joined + jnp.concatenate([pair[..., :HD], jnp.zeros_like(state)], axis=-1)
        pair = jnp.where(place >= width, joined, pair)
        width *= 2
    previous = shifted(pair, axis, 1)
    result = previous[..., :HD]
    if width + 1 < count:
        far_state = shifted(pair[..., :HD], axis, width + 1)
        result = result + jnp.einsum(
            "hij,hjk->hik", previous[..., HD:], far_state, precision=HIGH_PRECISION
        )
    return result


def step_pair(pair, inputs):
    return (pair_update(pair, inputs), pair)


def rim_from_behind(qkv_blocks, block_scales, head_share):
    outer_count = lax.axis_size("outer")
    inner_count = lax.axis_size("inner")
    token_count = qkv_blocks.shape[0]
    head_count = qkv_blocks.shape[1]
    quarter = qkv_blocks.shape[2] // 4
    tail = qkv_blocks[token_count - CONV + 1 :].astype(jnp.float32)
    tail = tail.reshape(CONV - 1, head_count, 4, quarter) * block_scales[-1].astype(
        jnp.float32
    )[None, :, :, None]
    tail = tail.reshape(CONV - 1, head_count, 4 * quarter)
    received = None
    for target in range(inner_count):
        piece = tail[:, target * head_share : (target + 1) * head_share]
        pairs = [
            ((block - 1) * inner_count + inner_count - 1, block * inner_count + target)
            for block in range(1, outer_count)
        ]
        got = lax.ppermute(piece, ("outer", "inner"), pairs)
        received = got if received is None else received + got
    return received


def local(qkv_blocks, block_scales, gate_logits, conv_weight, decay_log, dt_bias, norm_gain):
    inner_count = lax.axis_size("inner")
    own_tokens, head_count, channels = qkv_blocks.shape
    head_share = head_count // inner_count
    previous = rim_from_behind(qkv_blocks, block_scales, head_share)
    scale_rows = jnp.repeat(block_scales, QB, axis=0)
    extra = jnp.concatenate([scale_rows, gate_logits], axis=-1)
    extra_width = extra.shape[-1]
    extra_rows = own_tokens * extra_width // channels
    extra = jnp.swapaxes(extra, 0, 1).reshape(head_count, extra_rows, channels)
    packed = jnp.concatenate([qkv_blocks, jnp.swapaxes(extra, 0, 1)], axis=0)
    shared = lax.all_to_all(packed, "inner", split_axis=1, concat_axis=0, tiled=True)
    shared = shared.reshape(inner_count, own_tokens + extra_rows, head_share, channels)
    coded_share = shared[:, :own_tokens].reshape(inner_count * own_tokens, head_share, channels)
    extra_share = jnp.swapaxes(shared[:, own_tokens:], 1, 2).reshape(
        inner_count, head_share, own_tokens, extra_width
    )
    extra_share = jnp.swapaxes(extra_share, 1, 2).reshape(
        inner_count * own_tokens, head_share, extra_width
    )
    scale_share = extra_share[..., :4]
    gate_share = extra_share[..., 4:]
    token_count = coded_share.shape[0]
    quarter = channels // 4
    regrouped = (
        coded_share.astype(jnp.float32).reshape(token_count, head_share, 4, quarter)
        * scale_share.astype(jnp.float32)[..., None]
    ).reshape(token_count, head_share, channels)
    mixed = convolve(jnp.concatenate([previous, regrouped], axis=0), conv_weight, token_count)
    query_heads, key_heads, queries, keys_in, values_in, beta_gate, log_decay = split_heads(
        mixed, gate_share, decay_log, dt_bias
    )
    solved, attend, grown_query, carried_keys, decay_total = block_terms(
        query_heads, key_heads, queries, keys_in, values_in, beta_gate, log_decay
    )
    update_part = solved[..., :HD]
    write_part = solved[..., HD:]
    value_heads = queries.shape[1]
    zero_state = jnp.zeros((value_heads, HD, HD), jnp.float32)
    identity = jnp.broadcast_to(jnp.eye(HD, dtype=jnp.float32), (value_heads, HD, HD))
    start_pair = jnp.concatenate([zero_state, identity], axis=-1)
    sequence = (update_part, write_part, carried_keys, decay_total)
    final_pair, start_pairs = lax.scan(step_pair, start_pair, sequence)
    incoming = incoming_state(final_pair, "outer")
    attended = jnp.einsum("...ce,...ed->...cd", attend, solved, precision=HIGH_PRECISION)
    effective_query = grown_query - attended[..., HD:]
    through_state = jnp.einsum(
        "...ck,...kj->...cj", effective_query, start_pairs, precision=HIGH_PRECISION
    )
    local_part = attended[..., :HD] + through_state[..., :HD]
    outputs = local_part + jnp.einsum(
        "bhck,hkv->bhcv", through_state[..., HD:], incoming, precision=HIGH_PRECISION
    )
    scaled = (
        outputs
        * lax.rsqrt(jnp.mean(outputs * outputs, axis=-1, keepdims=True) + EPS_NORM)
        * norm_gain
    )
    normed = scaled.astype(jnp.bfloat16)
    by_token = jnp.swapaxes(normed, 1, 2).reshape(token_count, value_heads, HD)
    return lax.all_to_all(by_token, "inner", split_axis=0, concat_axis=1, tiled=True)


def solution(mesh):
    placed = (
        P(("outer", "inner"), None, None),
        P(("outer", "inner"), None, None),
        P(("outer", "inner"), None, None),
        P(None, "inner", None),
        P("inner"),
        P("inner"),
        P(),
    )
    return jax.shard_map(
        local,
        mesh=mesh,
        in_specs=placed,
        out_specs=P(("outer", "inner"), None, None),
        check_vma=False,
    )
```

profile of v0, /device:TPU:24, one launch (start us, length us, event | category | flops | bytes accessed | tf_op | source)
XLA Modules:
  0.0 288.0 jit_solution(1834936114891351251)
XLA Ops:
  2.1 2.8 copy.66
  4.9 1.7 pad_maximum_fusion.1
  6.6 4.6 %all-to-all-start = ((bf16[130,16,512]{2,0,1:T(8,128)(2,1)}), bf16[130,16,512]{2,0,1:T(8,128)(2,1)}, u32[]{:S(2)}, u32[]{:S(2)}) async-start(bf16[130,16,512]{2,0,1:T(8,128)(2,1)} %pad_maximum_fusion.1), calls=%async_computation | async-start | bytes 4456448 | tf_op jit(solution)/shard_map/all_to_all | solution.py:184
  14.1 1.8 collective-permute-start
  16.2 8.8 %collective-permute-done = f32[3,4,512]{2,0,1:T(4,128)S(1)} collective-permute-done((f32[3,4,512]{2,0,1:T(4,128)S(1)}, f32[3,4,512]{2,0,1:T(4,128)S(1)}, u32[]{:S(2)}, u32[]{:S(2)}) %collective-permute-start) | collective-permute-done | bytes 24608 | tf_op jit(solution)/shard_map/ppermute | solution.py:168
  25.1 13.7 %all-to-all-done = bf16[130,16,512]{2,0,1:T(8,128)(2,1)} async-done(((bf16[130,16,512]{2,0,1:T(8,128)(2,1)}), bf16[130,16,512]{2,0,1:T(8,128)(2,1)}, u32[]{:S(2)}, u32[]{:S(2)}) %all-to-all-start) | async-done | bytes 2129952 | tf_op jit(solution)/shard_map/all_to_all | solution.py:184
  42.2 4.2 %slice_convert_fusion = f32[4,128,4,512]{3,1,2,0:T(8,128)} fusion(bf16[4,130,4,512]{3,1,2,0:T(8,128)(2,1)} %bitcast.12), kind=kLoop, calls=%fused_computation.43 | loop fusion | flops 1048576 | bytes 6291456 | tf_op jit(solution)/shard_map/convert_element_type | solution.py:198
  46.8 4.8 %copy.72 = f32[4,128,4,512]{3,1,0,2:T(8,128)} copy(f32[4,128,4,512]{3,1,2,0:T(8,128)} %slice_convert_fusion) | data formatting | bytes 8388608 | tf_op jit(solution)/shard_map/convert_element_type | solution.py:198
  51.6 3.8 %mul.181 = f32[512,4,4,128]{3,2,0,1:T(4,128)} broadcast(f32[512,4,4]{2,0,1:T(8,128)S(1)} %copy.74), dimensions={0,1,2} | broadcast | bytes 4227072 | tf_op jit(solution)/shard_map/mul | solution.py:198
  55.4 5.5 %mul.182 = f32[512,4,512]{2,0,1:T(8,128)} reshape(f32[512,4,4,128]{3,2,0,1:T(4,128)} %mul.181) | data formatting | bytes 8388608 | tf_op jit(solution)/shard_map/mul | solution.py:198
  60.9 4.5 %bitcast_multiply_fusion = f32[512,4,512]{2,0,1:T(8,128)S(1)} fusion(f32[512,4,512]{2,0,1:T(8,128)} %mul.182, f32[4,128,4,512]{3,1,0,2:T(8,128)} %copy.72), kind=kLoop, calls=%fused_computation.28 | loop fusion | flops 1048576 | bytes 12582912 | tf_op jit(solution)/shard_map/mul | solution.py:198
  65.3 2.5 divide_multiply_fusion
  71.2 1.9 reshape_reshape.9
  73.1 2.0 slice_multiply_fusion.3
  76.4 2.0 fusion.27
  80.3 2.7 broadcast_add_fusion
  83.0 2.9 %copy.79 = f32[4,8,128,128]{2,3,1,0:T(8,128)} copy(f32[4,8,128,128]{3,2,1,0:T(8,128)} %get-tuple-element.125) | data formatting | bytes 4194304 | tf_op jit(solution)/shard_map/while | solution.py:68
  85.9 53.3 %while.24 = (s32[]{:T(128)}, f32[4,8,128,128]{2,3,1,0:T(8,128)}, f32[4,8,128,128]{3,2,1,0:T(8,128)S(1)}, s32[]{:T(128)}) while((s32[]{:T(128)}, f32[4,8,128,128]{2,3,1,0:T(8,128)}, f32[4,8,128,128]{3,2,1,0:T(8,128)S(1)}, s32[]{:T(128)}) %tuple.58), condition=%wide.region_4.5_spmd, body=%wide.region_3.4_spmd.sunk | while | flops 1611137024 | bytes 18874420 | solution.py:68
  86.1 1.6 copy.135
  87.8 2.1 fusion.90
  89.9 5.0 %bitcast_add_fusion.2 = f32[4,8,128,128]{2,3,1,0:T(8,128)} fusion(f32[4,8,128,128]{2,3,1,0:T(8,128)S(1)} %copy.135, f32[4,8,128,128]{3,2,1,0:T(8,128)S(1)} %fusion.90), kind=kOutput, calls=%fused_computation.clone.1 | convolution fusion | flops 805830656 | bytes 6291456 | tf_op jit(solution)/shard_map/while/body/eval_jaxpr/...ij,...jk->...ik/dot_general | solution.py:62
  96.7 2.1 fusion.90
  98.8 5.0 %bitcast_add_fusion.2 = f32[4,8,128,128]{2,3,1,0:T(8,128)} fusion(f32[4,8,128,128]{2,3,1,0:T(8,128)S(1)} %copy.135, f32[4,8,128,128]{3,2,1,0:T(8,128)S(1)} %fusion.90), kind=kOutput, calls=%fused_computation.clone.1 | convolution fusion | flops 805830656 | bytes 6291456 | tf_op jit(solution)/shard_map/while/body/eval_jaxpr/...ij,...jk->...ik/dot_general | solution.py:62
  105.5 2.1 fusion.90
  107.7 5.0 %bitcast_add_fusion.2 = f32[4,8,128,128]{2,3,1,0:T(8,128)} fusion(f32[4,8,128,128]{2,3,1,0:T(8,128)S(1)} %copy.135, f32[4,8,128,128]{3,2,1,0:T(8,128)S(1)} %fusion.90), kind=kOutput, calls=%fused_computation.clone.1 | convolution fusion | flops 805830656 | bytes 6291456 | tf_op jit(solution)/shard_map/while/body/eval_jaxpr/...ij,...jk->...ik/dot_general | solution.py:62
  114.4 2.1 fusion.90
  116.5 5.0 %bitcast_add_fusion.2 = f32[4,8,128,128]{2,3,1,0:T(8,128)} fusion(f32[4,8,128,128]{2,3,1,0:T(8,128)S(1)} %copy.135, f32[4,8,128,128]{3,2,1,0:T(8,128)S(1)} %fusion.90), kind=kOutput, calls=%fused_computation.clone.1 | convolution fusion | flops 805830656 | bytes 6291456 | tf_op jit(solution)/shard_map/while/body/eval_jaxpr/...ij,...jk->...ik/dot_general | solution.py:62
  123.2 2.1 fusion.90
  125.4 5.0 %bitcast_add_fusion.2 = f32[4,8,128,128]{2,3,1,0:T(8,128)} fusion(f32[4,8,128,128]{2,3,1,0:T(8,128)S(1)} %copy.135, f32[4,8,128,128]{3,2,1,0:T(8,128)S(1)} %fusion.90), kind=kOutput, calls=%fused_computation.clone.1 | convolution fusion | flops 805830656 | bytes 6291456 | tf_op jit(solution)/shard_map/while/body/eval_jaxpr/...ij,...jk->...ik/dot_general | solution.py:62
  132.1 2.1 fusion.90
  134.2 5.0 %bitcast_add_fusion.2 = f32[4,8,128,128]{2,3,1,0:T(8,128)} fusion(f32[4,8,128,128]{2,3,1,0:T(8,128)S(1)} %copy.135, f32[4,8,128,128]{3,2,1,0:T(8,128)S(1)} %fusion.90), kind=kOutput, calls=%fused_computation.clone.1 | convolution fusion | flops 805830656 | bytes 6291456 | tf_op jit(solution)/shard_map/while/body/eval_jaxpr/...ij,...jk->...ik/dot_general | solution.py:62
  142.8 3.8 %fusion.15 = f32[4,8,128,256]{3,2,1,0:T(8,128)S(1)} fusion(f32[4,8,128,128]{2,3,1,0:T(8,128)S(1)} %copy-done, f32[4,8,128,128]{3,2,1,0:T(8,128)S(1)} %get-tuple-element.131, f32[4,8,128,128]{3,2,1,0:T(8,128)S(1)} %copy-done.7), kind=kOutput, calls=%fused_computation.24 | convolution fusion | flops 1611661312 | bytes 10485760 | tf_op jit(solution)/shard_map/...ce,...ed->...cd/dot_general | solution.py:90
  146.6 2.8 fusion.59
  149.8 23.0 %while.25 = (s32[]{:T(128)}, f32[8,128,256]{2,1,0:T(8,128)S(1)}, f32[4,8,128,256]{3,2,1,0:T(8,128)}, f32[4,8]{1,0:T(4,128)S(1)}, f32[4,8,128,128]{3,2,1,0:T(8,12...) while((s32[]{:T(128)}, f32[8,128,256]{2,1,0:T(8,128)S(1)}, ...), condition=%wide.region_6.7_spmd, body=%wide.region_5.6_spmd.sunk | while | flops 806092800 | bytes 9962161 | solution.py:215
  151.1 2.1 convolution_subtract_fusion.2
  156.9 2.1 convolution_subtract_fusion.2
  162.6 2.1 convolution_subtract_fusion.2
  168.3 2.1 convolution_subtract_fusion.2
  172.9 3.7 %collective-permute-start.4 = (f32[8,128,256]{2,1,0:T(8,128)S(1)}, f32[8,128,256]{2,1,0:T(8,128)S(1)}, u32[]{:S(2)}, u32[]{:S(2)}) collective-permute-start(f32[8,128,256]{2,1,0:T(8,128)S(1)} %get-tuple-element.62), channel_id=1, source_target_pairs={{0,4},{4,8},{8,12},{12,16},{16,20},{20,24},{24,28},{1,5},{5,9},{9,... | collective-permute-start | bytes 3145736 | tf_op jit(solution)/shard_map/ppermute | solution.py:120
  176.6 23.4 %collective-permute-done.4 = f32[8,128,256]{2,1,0:T(8,128)S(1)} collective-permute-done((f32[8,128,256]{2,1,0:T(8,128)S(1)}, f32[8,128,256]{2,1,0:T(8,128)S(1)}, u32[]{:S(2)}, u32[]{:S(2)}) %collective-permute-start.4) | collective-permute-done | bytes 1048608 | tf_op jit(solution)/shard_map/ppermute | solution.py:120
  202.3 23.9 %collective-permute-done.5 = f32[8,128,256]{2,1,0:T(8,128)S(1)} collective-permute-done((f32[8,128,256]{2,1,0:T(8,128)S(1)}, f32[8,128,256]{2,1,0:T(8,128)S(1)}, u32[]{:S(2)}, u32[]{:S(2)}) %collective-permute-start.5) | collective-permute-done | bytes 1048608 | tf_op jit(solution)/shard_map/ppermute | solution.py:120
  227.3 3.9 %collective-permute-start.6 = (f32[8,128,256]{2,1,0:T(8,128)S(1)}, f32[8,128,256]{2,1,0:T(8,128)S(1)}, u32[]{:S(2)}, u32[]{:S(2)}) collective-permute-start(f32[8,128,256]{2,1,0:T(8,128)S(1)} %fusion.34), channel_id=1, source_target_pairs={{0,4},{4,8},{8,12},{12,16},{16,20},{20,24},{24,28},{1,5},{5,9},{9,... | collective-permute-start | bytes 3145736 | tf_op jit(solution)/shard_map/ppermute | solution.py:120
  231.2 7.5 %fusion.26 = f32[4,8,128,256]{3,2,1,0:T(8,128)S(1)} fusion(f32[4,8,128,256]{3,2,1,0:T(8,128)} %copy-done.1, f32[4,8,256,128]{3,2,1,0:T(8,128)} %bitcast.135, f32[4,8,128]{2,1,0:T(8,128)S(1)} %reduce_window_sum.11, pred[128,128]{1,0:T(8,128)(4,1)S(1)} %get-tuple-element.154), kind=kOutput, calls=%fused_computation.42 | convolution fusion | flops 1612709888 | bytes 10534912 | tf_op jit(solution)/shard_map/...ce,...ed->...cd/dot_general | solution.py:217
  238.7 1.8 collective-permute-start.7
  240.9 4.5 %fusion.22 = f32[4,8,128,256]{3,2,1,0:T(8,128)S(1)} fusion(f32[4,8,128,256]{3,2,1,0:T(8,128)S(1)} %copy-done.9, f32[4,8,128,256]{3,2,1,0:T(8,128)S(1)} %fusion.26, f32[4,128,8,128]{3,1,0,2:T(8,128)S(1)} %bitcast.139, f32[4,8,128]{2,1,0:T(8,128)S(1)} %get-tuple-element.145), kind=kOutput, calls=%fused_computation.36 | convolution fusion | flops 1611661312 | bytes 12599296 | tf_op jit(solution)/shard_map/...ck,...kj->...cj/dot_general | solution.py:219
  245.4 18.4 %collective-permute-done.7 = f32[8,128,128]{2,1,0:T(8,128)S(1)} collective-permute-done((f32[8,128,128]{2,1,0:T(8,128)S(1)}, f32[8,128,128]{2,1,0:T(8,128)S(1)}, u32[]{:S(2)}, u32[]{:S(2)}) %collective-permute-start.7) | collective-permute-done | bytes 524320 | tf_op jit(solution)/shard_map/ppermute | solution.py:120
  264.5 2.8 multiply_reduce_fusion
  268.7 17.8 %all_to_all.33 = bf16[512,8,128]{2,1,0:T(8,128)(2,1)S(1)} all-to-all(bf16[512,8,128]{2,1,0:T(8,128)(2,1)S(1)} %bitcast.140), channel_id=1, replica_groups=mesh['outer'=8,'inner'=4] {'inner'}, dimensions={0} | all-to-all | bytes 2097152 | tf_op jit(solution)/shard_map/all_to_all | solution.py:233
  (119 shorter events, 49.8 us)
Async XLA Ops:
  6.6 9.4 %copy-start.14 = (f32[8]{0:T(128)S(1)}, f32[8]{0:T(128)}, u32[]{:S(2)}) copy-start(f32[8]{0:T(128)} %param.15) | copy-start | bytes 100
  6.6 9.5 %copy-start.10 = (f32[4,4,512]{2,1,0:T(4,128)S(1)}, f32[4,4,512]{2,1,0:T(4,128)}, u32[]{:S(2)}) copy-start(f32[4,4,512]{2,1,0:T(4,128)} %param.14) | copy-start | bytes 98308
  6.6 32.2 %all-to-all-start = ((bf16[130,16,512]{2,0,1:T(8,128)(2,1)}), bf16[130,16,512]{2,0,1:T(8,128)(2,1)}, u32[]{:S(2)}, u32[]{:S(2)}) async-start(bf16[130,16,512]{2,0,1:T(8,128)(2,1)} %pad_maximum_fusion.1), calls=%async_computation | async-start | bytes 4456448 | tf_op jit(solution)/shard_map/all_to_all | solution.py:184
  12.1 28.6 %copy-start.12 = (f32[8]{0:T(128)S(1)}, f32[8]{0:T(128)}, u32[]{:S(2)}) copy-start(f32[8]{0:T(128)} %param.16) | copy-start | bytes 100
  12.1 4.1 %collective-permute-start.1 = (f32[3,4,512]{2,0,1:T(4,128)S(1)}, f32[3,4,512]{2,0,1:T(4,128)S(1)}, u32[]{:S(2)}, u32[]{:S(2)}) collective-permute-start(f32[3,4,512]{2,0,1:T(4,128)S(1)} %get-tuple-element.133), channel_id=1, source_target_pairs={{3,5},{7,9},{11,13},{15,17},{19,21},{23,25},{27,29}} | collective-permute-start | bytes 73736 | tf_op jit(solution)/shard_map/ppermute | solution.py:168
  12.8 3.4 %collective-permute-start.3 = (f32[3,4,512]{2,0,1:T(4,128)S(1)}, f32[3,4,512]{2,0,1:T(4,128)S(1)}, u32[]{:S(2)}, u32[]{:S(2)}) collective-permute-start(f32[3,4,512]{2,0,1:T(4,128)S(1)} %get-tuple-element.134), channel_id=1, source_target_pairs={{3,7},{7,11},{11,15},{15,19},{19,23},{23,27},{27,31}} | collective-permute-start | bytes 73736 | tf_op jit(solution)/shard_map/ppermute | solution.py:168
  13.5 2.8 collective-permute-start.2
  14.1 10.9 %collective-permute-start = (f32[3,4,512]{2,0,1:T(4,128)S(1)}, f32[3,4,512]{2,0,1:T(4,128)S(1)}, u32[]{:S(2)}, u32[]{:S(2)}) collective-permute-start(f32[3,4,512]{2,0,1:T(4,128)S(1)} %get-tuple-element.136), channel_id=1, source_target_pairs={{3,4},{7,8},{11,12},{15,16},{19,20},{23,24},{27,28}} | collective-permute-start | bytes 73736 | tf_op jit(solution)/shard_map/ppermute | solution.py:168
  67.9 2.0 copy-start.2
  75.1 1.0 copy-start.4
  75.1 1.3 copy-start.6
  78.4 1.9 copy-start.8
  78.9 4.1 %copy-start.3 = (f32[4,4,2,256,128]{4,3,2,1,0:T(8,128)}, f32[4,4,2,256,128]{4,3,2,1,0:T(8,128)S(1)}, u32[]{:S(2)}) copy-start(f32[4,4,2,256,128]{4,3,2,1,0:T(8,128)S(1)} %broadcast_in_dim.56) | copy-start | bytes 12582916
  140.6 1.6 copy-start
  140.6 2.2 copy-start.7
  146.6 3.2 %copy-start.1 = (f32[4,8,128,256]{3,2,1,0:T(8,128)}, f32[4,8,128,256]{3,2,1,0:T(8,128)S(1)}, u32[]{:S(2)}) copy-start(f32[4,8,128,256]{3,2,1,0:T(8,128)S(1)} %fusion.15) | copy-start | bytes 12582916
  149.8 50.1 %copy-start.11 = (pred[256]{0:T(512)(128)(4,1)S(1)}, pred[256]{0:T(512)(128)(4,1)}, u32[]{:S(2)}) copy-start(pred[256]{0:T(512)(128)(4,1)} %constant.51.clone.1) | copy-start | bytes 772
  172.9 27.0 %collective-permute-start.4 = (f32[8,128,256]{2,1,0:T(8,128)S(1)}, f32[8,128,256]{2,1,0:T(8,128)S(1)}, u32[]{:S(2)}, u32[]{:S(2)}) collective-permute-start(f32[8,128,256]{2,1,0:T(8,128)S(1)} %get-tuple-element.62), channel_id=1, source_target_pairs={{0,4},{4,8},{8,12},{12,16},{16,20},{20,24},{24,28},{1,5},{5,9},{9,... | collective-permute-start | bytes 3145736 | tf_op jit(solution)/shard_map/ppermute | solution.py:120
  201.0 25.2 %collective-permute-start.5 = (f32[8,128,256]{2,1,0:T(8,128)S(1)}, f32[8,128,256]{2,1,0:T(8,128)S(1)}, u32[]{:S(2)}, u32[]{:S(2)}) collective-permute-start(f32[8,128,256]{2,1,0:T(8,128)S(1)} %fusion.35), channel_id=1, source_target_pairs={{0,8},{4,12},{8,16},{12,20},{16,24},{20,28},{1,9},{5,13},{9,17},{1... | collective-permute-start | bytes 3145736 | tf_op jit(solution)/shard_map/ppermute | solution.py:120
  227.3 13.2 %copy-start.5 = (f32[512,4,128]{2,0,1:T(8,128)S(1)}, f32[512,4,128]{2,0,1:T(8,128)}, u32[]{:S(2)}) copy-start(f32[512,4,128]{2,0,1:T(8,128)} %copy-done.4) | copy-start | bytes 3145732
  227.3 36.5 %collective-permute-start.6 = (f32[8,128,256]{2,1,0:T(8,128)S(1)}, f32[8,128,256]{2,1,0:T(8,128)S(1)}, u32[]{:S(2)}, u32[]{:S(2)}) collective-permute-start(f32[8,128,256]{2,1,0:T(8,128)S(1)} %fusion.34), channel_id=1, source_target_pairs={{0,4},{4,8},{8,12},{12,16},{16,20},{20,24},{24,28},{1,5},{5,9},{9,... | collective-permute-start | bytes 3145736 | tf_op jit(solution)/shard_map/ppermute | solution.py:120
  238.7 2.2 copy-start.9
  238.7 25.0 %collective-permute-start.7 = (f32[8,128,128]{2,1,0:T(8,128)S(1)}, f32[8,128,128]{2,1,0:T(8,128)S(1)}, u32[]{:S(2)}, u32[]{:S(2)}) collective-permute-start(f32[8,128,128]{2,1,0:T(8,128)S(1)} %slice.177), channel_id=1, source_target_pairs={{0,20},{4,24},{8,28},{1,21},{5,25},{9,29},{2,22},{6,26},{10,30},{3... | collective-permute-start | bytes 1572872 | tf_op jit(solution)/shard_map/ppermute | solution.py:120
  264.5 2.8 copy-start.13
where the time goes:
time: 292 us; the launch traced here: 288 us
  waiting for transfers between devices  88.3 us (30%)
  matrix products  80.2 us (27%)
  local copies, waits for them, and re-layouts  58.3 us (20%)
  other arithmetic  22.9 us (8%)
  starting transfers between devices  19 us (7%)
  blocking collectives  17.8 us (6%)
    ppermute x4, waiting for transfers between devices, shifted(): lax.ppermute(value, axis, [(source, source + steps) for source in range(c...  65.7 us
    dot_general x6, matrix products, level(): jnp.einsum('...ij,...jk->...ik', inverse, power, precision=HIGH_PRECISION)  29.9 us
    all_to_all x1, blocking collectives, local(): lax.all_to_all(by_token, 'inner', split_axis=0, concat_axis=1, tiled=True)  17.8 us
    all_to_all x1, waiting for transfers between devices, local(): lax.all_to_all(packed, 'inner', split_axis=1, concat_axis=0, tiled=True)  13.7 us
    dot_general x6, matrix products, level(): jnp.einsum('...ij,...jk->...ik', power, power, precision=HIGH_PRECISION)  12.8 us
    ppermute x4, starting transfers between devices, shifted(): lax.ppermute(value, axis, [(source, source + steps) for source in range(c...  10.6 us
    while x12, local copies, waits for them, and re-layouts  10.4 us
    mul x2, local copies, waits for them, and re-layouts, local(): coded_share.astype(jnp.float32).reshape(token_count, head_share, 4, quarter)  9.31 us
  transfers between devices with their start and end apart: 9, of which 6 were waited for; matrix products, arithmetic and copies ran while one was open for 5% of the time, Pallas kernels for 0%

commit v1 on v0

--- a/solution.py
+++ b/solution.py
@@ -55,17 +55,14 @@
 def lower_inverse(strict_part, length):
     negated = -strict_part
     eye_block = jnp.eye(length, dtype=jnp.float32)
-
-    def level(unused_level, carried):
-        inverse, power = carried
+    inverse = eye_block + negated
+    power = negated
+    for unused_level in range((length - 1).bit_length() - 1):
         power = jnp.einsum("...ij,...jk->...ik", power, power, precision=HIGH_PRECISION)
         inverse = inverse + jnp.einsum(
             "...ij,...jk->...ik", inverse, power, precision=HIGH_PRECISION
         )
-        return (inverse, power)
-
-    levels = (length - 1).bit_length() - 1
-    return lax.fori_loop(0, levels, level, (eye_block + negated, negated))[0]
+    return inverse
 
 
 def block_terms(query_heads, key_heads, queries, keys_in, values_in, beta_gate, log_decay):

time: 292 us -> 267 us (0.914)
  local copies, waits for them, and re-layouts: 58.3 us -> 44 us
  matrix products: 80.2 us -> 70.8 us
    while x13 -> x0, local copies, waits for them, and re-layouts: 13.3 us -> none
    dot_general x12, matrix products: 42.7 us -> 32.6 us  [the longest x6 18.3 us: lower_inverse(): jnp.einsum('...ij,...jk->...ik', inverse, power, precision=HIGH_PRECISION)]
    unnamed x33 -> x31, local copies, waits for them, and re-layouts: 8.87 us -> 6.62 us
where the time goes in v1:
time: 267 us; the launch traced here: 263 us
  waiting for transfers between devices  88.8 us (33%)
  matrix products  70.8 us (27%)
  local copies, waits for them, and re-layouts  44 us (16%)
  other arithmetic  21.3 us (8%)
  starting transfers between devices  18.5 us (7%)
  blocking collectives  17.8 us (7%)
    ppermute x4, waiting for transfers between devices, shifted(): lax.ppermute(value, axis, [(source, source + steps) for source in range(c...  65.7 us
    dot_general x6, matrix products, lower_inverse(): jnp.einsum('...ij,...jk->...ik', inverse, power, precision=HIGH_PRECISION)  18.3 us
    all_to_all x1, blocking collectives, local(): lax.all_to_all(by_token, 'inner', split_axis=0, concat_axis=1, tiled=True)  17.8 us
    dot_general x6, matrix products, lower_inverse(): jnp.einsum('...ij,...jk->...ik', power, power, precision=HIGH_PRECISION)  14.2 us
    all_to_all x1, waiting for transfers between devices, local(): lax.all_to_all(packed, 'inner', split_axis=1, concat_axis=0, tiled=True)  13.7 us
    ppermute x4, starting transfers between devices, shifted(): lax.ppermute(value, axis, [(source, source + steps) for source in range(c...  10.6 us
    ppermute x4, waiting for transfers between devices, rim_from_behind(): got = lax.ppermute(piece, ('outer', 'inner'), pairs)  9.37 us
    mul x2, local copies, waits for them, and re-layouts, local(): coded_share.astype(jnp.float32).reshape(token_count, head_share, 4, quarter)  9.32 us
  transfers between devices with their start and end apart: 9, of which 6 were waited for; matrix products, arithmetic and copies ran while one was open for 5% of the time, Pallas kernels for 0%

profile of v1, /device:TPU:24, one launch (start us, length us, event | category | flops | bytes accessed | tf_op | source)
XLA Modules:
  0.0 262.5 jit_solution(11161506859557381000)
XLA Ops:
  2.1 2.8 %copy.52 = bf16[128,16,512]{2,0,1:T(8,128)(2,1)S(1)} copy(bf16[128,16,512]{2,1,0:T(8,128)(2,1)} %param.9) | data formatting | bytes 4194304 | tf_op args[0]
  4.9 1.6 pad_maximum_fusion.1
  6.5 4.6 %all-to-all-start = ((bf16[130,16,512]{2,0,1:T(8,128)(2,1)}), bf16[130,16,512]{2,0,1:T(8,128)(2,1)}, u32[]{:S(2)}, u32[]{:S(2)}) async-start(bf16[130,16,512]{2,0,1:T(8,128)(2,1)} %pad_maximum_fusion.1), calls=%async_computation | async-start | bytes 4456448 | tf_op jit(solution)/shard_map/all_to_all | solution.py:181
  15.7 9.4 %collective-permute-done = f32[3,4,512]{2,0,1:T(4,128)S(1)} collective-permute-done((f32[3,4,512]{2,0,1:T(4,128)S(1)}, f32[3,4,512]{2,0,1:T(4,128)S(1)}, u32[]{:S(2)}, u32[]{:S(2)}) %collective-permute-start) | collective-permute-done | bytes 24608 | tf_op jit(solution)/shard_map/ppermute | solution.py:165
  25.1 13.7 %all-to-all-done = bf16[130,16,512]{2,0,1:T(8,128)(2,1)} async-done(((bf16[130,16,512]{2,0,1:T(8,128)(2,1)}), bf16[130,16,512]{2,0,1:T(8,128)(2,1)}, u32[]{:S(2)}, u32[]{:S(2)}) %all-to-all-start) | async-done | bytes 2129952 | tf_op jit(solution)/shard_map/all_to_all | solution.py:181
  42.4 4.2 %slice_convert_fusion = f32[4,128,4,512]{3,1,2,0:T(8,128)} fusion(bf16[4,130,4,512]{3,1,2,0:T(8,128)(2,1)} %bitcast.11), kind=kLoop, calls=%fused_computation.42 | loop fusion | flops 1048576 | bytes 6291456 | tf_op jit(solution)/shard_map/convert_element_type | solution.py:195
  46.9 4.7 %copy.58 = f32[4,128,4,512]{3,1,0,2:T(8,128)} copy(f32[4,128,4,512]{3,1,2,0:T(8,128)} %slice_convert_fusion) | data formatting | bytes 8388608 | tf_op jit(solution)/shard_map/convert_element_type | solution.py:195
  51.7 3.8 %mul.181 = f32[512,4,4,128]{3,2,0,1:T(4,128)} broadcast(f32[512,4,4]{2,0,1:T(8,128)S(1)} %copy.60), dimensions={0,1,2} | broadcast | bytes 4227072 | tf_op jit(solution)/shard_map/mul | solution.py:195
  55.5 5.5 %mul.182 = f32[512,4,512]{2,0,1:T(8,128)} reshape(f32[512,4,4,128]{3,2,0,1:T(4,128)} %mul.181) | data formatting | bytes 8388608 | tf_op jit(solution)/shard_map/mul | solution.py:195
  61.0 4.5 %bitcast_multiply_fusion = f32[512,4,512]{2,0,1:T(8,128)S(1)} fusion(f32[512,4,512]{2,0,1:T(8,128)} %mul.182, f32[4,128,4,512]{3,1,0,2:T(8,128)} %copy.58), kind=kLoop, calls=%fused_computation.27 | loop fusion | flops 1048576 | bytes 12582912 | tf_op jit(solution)/shard_map/mul | solution.py:195
  65.5 2.5 divide_multiply_fusion
  72.0 2.0 fusion.27
  74.5 4.0 %fusion.50 = f32[4,8,128,128]{3,2,1,0:T(8,128)S(1)} fusion(f32[4,8,256,128]{3,2,1,0:T(8,128)S(1)} %bitcast.136, f32[4,8,128]{2,1,0:T(8,128)S(1)} %bitcast.151, f32[4,8,128]{2,1,0:T(8,128)S(1)} %reduce_window_sum.11, pred[128,128]{1,0:T(8,128)(4,1)S(1)} %get-tuple-element.114, pred[128,128]{1,0:T(8,128)(4,1)S(1)} %get-tuple-element.115), kind=kOutput, calls=%fused_computation.81 | convolution fusion | flops 808976384 | bytes 4276224 | tf_op jit(solution)/shard_map/...ij,...jk->...ik/dot_general | solution.py:61
  78.5 6.9 %add_add_fusion = f32[4,8,128,128]{3,2,1,0:T(8,128)} fusion(f32[4,8,128,128]{3,2,1,0:T(8,128)S(1)} %fusion.50, f32[128,128]{1,0:T(8,128)S(1)} %fusion.59, f32[4,8,128]{2,1,0:T(8,128)S(1)} %bitcast.152, f32[4,8,128]{2,1,0:T(8,128)S(1)} %reduce_window_sum.11, pred[128,128]{1,0:T(8,128)(4,1)S(1)} %get-tuple-element.115, f32[4,8,256,128]{3,2,1,0:T(8,128)S(1)} %bitcast.137, ...), kind=kOutput, calls=%fused_computation.56 | convolution fusion | flops 814219264 | bytes 8683520 | tf_op jit(solution)/shard_map/...ij,...jk->...ik/dot_general | solution.py:62
  85.5 2.1 fusion.74
  87.6 2.7 %copy.65 = f32[512,4,256]{2,1,0:T(4,128)} copy(f32[512,4,256]{2,0,1:T(8,128)S(1)} %slice-done) | data formatting | bytes 4194304 | tf_op jit(solution)/shard_map/slice | solution.py:35
  90.3 3.1 %reshape_reshape.9 = f32[4,128,8,128]{3,2,1,0:T(8,128)} reshape(f32[512,4,256]{2,1,0:T(4,128)} %copy.65) | data formatting | bytes 4194304 | tf_op jit(solution)/shard_map/reshape;reshape | solution.py:42
  93.4 2.1 bitcast_multiply_fusion.5
  95.6 2.0 fusion.76
  97.6 2.2 fusion.75
  99.8 2.0 fusion.77
  101.8 2.3 convolution_add_fusion.2
  104.1 2.0 fusion.79
  106.2 2.3 fusion.78
  108.5 2.0 fusion.80
  110.6 2.4 convolution_add_fusion.1
  113.0 2.2 fusion.81
  116.6 4.5 %fusion.15 = f32[4,8,128,256]{3,2,1,0:T(8,128)S(1)} fusion(f32[4,8,128,128]{3,2,1,0:T(8,128)S(1)} %get-tuple-element.93, f32[4,8,128,128]{3,2,1,0:T(8,128)S(1)} %bitcast_multiply_fusion.5, f32[4,8,128,128]{3,2,1,0:T(8,128)S(1)} %convolution_add_fusion.1, f32[4,8,128,128]{3,2,1,0:T(8,128)S(1)} %fusion.81), kind=kOutput, calls=%fused_computation.23 | convolution fusion | flops 1612185600 | bytes 12582912 | tf_op jit(solution)/shard_map/...ce,...ed->...cd/dot_general | solution.py:87
  121.1 2.8 %fusion.71 = (f32[4,8,128,128]{3,2,1,0:T(8,128)}, f32[4,8,128,128]{3,2,1,0:T(8,128)}) fusion(f32[4,8,128,256]{3,2,1,0:T(8,128)S(1)} %fusion.15), kind=kLoop, calls=%fused_computation.124 | loop fusion | bytes 8388608 | tf_op jit(solution)/shard_map/slice | solution.py:206
  124.3 22.9 %while.12 = (s32[]{:T(128)}, f32[8,128,256]{2,1,0:T(8,128)S(1)}, f32[4,8,128,256]{3,2,1,0:T(8,128)}, f32[4,8]{1,0:T(4,128)S(1)}, f32[4,8,128,128]{3,2,1,0:T(8,12...) while((s32[]{:T(128)}, f32[8,128,256]{2,1,0:T(8,128)S(1)}, ...), condition=%wide.region_4.5_spmd, body=%wide.region_3.4_spmd.sunk | while | flops 806092800 | bytes 9962161 | solution.py:212
  125.4 2.1 convolution_subtract_fusion.2
  128.6 1.5 convolution_add_fusion.6
  131.2 2.1 convolution_subtract_fusion.2
  134.3 1.5 convolution_add_fusion.6
  136.9 2.1 convolution_subtract_fusion.2
  140.0 1.5 convolution_add_fusion.6
  142.6 2.1 convolution_subtract_fusion.2
  145.8 1.5 convolution_add_fusion.6
  147.3 3.7 %collective-permute-start.4 = (f32[8,128,256]{2,1,0:T(8,128)S(1)}, f32[8,128,256]{2,1,0:T(8,128)S(1)}, u32[]{:S(2)}, u32[]{:S(2)}) collective-permute-start(f32[8,128,256]{2,1,0:T(8,128)S(1)} %get-tuple-element.44), channel_id=1, source_target_pairs={{0,4},{4,8},{8,12},{12,16},{16,20},{20,24},{24,28},{1,5},{5,9},{9,... | collective-permute-start | bytes 3145736 | tf_op jit(solution)/shard_map/ppermute | solution.py:117
  150.9 23.4 %collective-permute-done.4 = f32[8,128,256]{2,1,0:T(8,128)S(1)} collective-permute-done((f32[8,128,256]{2,1,0:T(8,128)S(1)}, f32[8,128,256]{2,1,0:T(8,128)S(1)}, u32[]{:S(2)}, u32[]{:S(2)}) %collective-permute-start.4) | collective-permute-done | bytes 1048608 | tf_op jit(solution)/shard_map/ppermute | solution.py:117
  176.7 23.9 %collective-permute-done.5 = f32[8,128,256]{2,1,0:T(8,128)S(1)} collective-permute-done((f32[8,128,256]{2,1,0:T(8,128)S(1)}, f32[8,128,256]{2,1,0:T(8,128)S(1)}, u32[]{:S(2)}, u32[]{:S(2)}) %collective-permute-start.5) | collective-permute-done | bytes 1048608 | tf_op jit(solution)/shard_map/ppermute | solution.py:117
  201.7 3.9 %collective-permute-start.6 = (f32[8,128,256]{2,1,0:T(8,128)S(1)}, f32[8,128,256]{2,1,0:T(8,128)S(1)}, u32[]{:S(2)}, u32[]{:S(2)}) collective-permute-start(f32[8,128,256]{2,1,0:T(8,128)S(1)} %fusion.41), channel_id=1, source_target_pairs={{0,4},{4,8},{8,12},{12,16},{16,20},{20,24},{24,28},{1,5},{5,9},{9,... | collective-permute-start | bytes 3145736 | tf_op jit(solution)/shard_map/ppermute | solution.py:117
  205.6 7.5 %fusion.26 = f32[4,8,128,256]{3,2,1,0:T(8,128)S(1)} fusion(f32[4,8,128,256]{3,2,1,0:T(8,128)} %copy-done, f32[4,8,256,128]{3,2,1,0:T(8,128)} %bitcast.138, f32[4,8,128]{2,1,0:T(8,128)S(1)} %reduce_window_sum.11, pred[128,128]{1,0:T(8,128)(4,1)S(1)} %get-tuple-element.115), kind=kOutput, calls=%fused_computation.41 | convolution fusion | flops 1612709888 | bytes 10534912 | tf_op jit(solution)/shard_map/...ce,...ed->...cd/dot_general | solution.py:214
  213.1 1.8 collective-permute-start.7
  215.2 4.5 %fusion.22 = f32[4,8,128,256]{3,2,1,0:T(8,128)S(1)} fusion(f32[4,8,128,256]{3,2,1,0:T(8,128)S(1)} %copy-done.8, f32[4,8,128,256]{3,2,1,0:T(8,128)S(1)} %fusion.26, f32[4,128,8,128]{3,1,0,2:T(8,128)S(1)} %bitcast.142, f32[4,8,128]{2,1,0:T(8,128)S(1)} %get-tuple-element.107), kind=kOutput, calls=%fused_computation.35 | convolution fusion | flops 1611661312 | bytes 12599296 | tf_op jit(solution)/shard_map/...ck,...kj->...cj/dot_general | solution.py:216
  219.8 18.4 %collective-permute-done.7 = f32[8,128,128]{2,1,0:T(8,128)S(1)} collective-permute-done((f32[8,128,128]{2,1,0:T(8,128)S(1)}, f32[8,128,128]{2,1,0:T(8,128)S(1)}, u32[]{:S(2)}, u32[]{:S(2)}) %collective-permute-start.7) | collective-permute-done | bytes 524320 | tf_op jit(solution)/shard_map/ppermute | solution.py:117
  238.9 2.7 %multiply_reduce_fusion = (f32[4,8,128]{2,1,0:T(8,128)S(1)}, f32[4,8,128,128]{3,2,1,0:T(8,128)S(1)}) fusion(f32[4,8,128,256]{3,2,1,0:T(8,128)S(1)} %fusion.22, f32[8,128,128]{2,1,0:T(8,128)S(1)} %fusion.53, f32[8,128,256]{2,1,0:T(8,128)S(1)} %collective-permute-done.6, f32[4,8,128,256]{3,2,1,0:T(8,128)S(1)} %fusion.26), kind=kOutput, calls=%fused_computation.53 | convolution fusion | flops 807530496 | bytes 9453568 | tf_op jit(solution)/shard_map/bhck,hkv->bhcv/dot_general | solution.py:220
  243.1 17.8 %all_to_all.33 = bf16[512,8,128]{2,1,0:T(8,128)(2,1)S(1)} all-to-all(bf16[512,8,128]{2,1,0:T(8,128)(2,1)S(1)} %bitcast.143), channel_id=1, replica_groups=mesh['outer'=8,'inner'=4] {'inner'}, dimensions={0} | all-to-all | bytes 2097152 | tf_op jit(solution)/shard_map/all_to_all | solution.py:230
  (104 shorter events, 32.3 us)
Async XLA Ops:
  6.5 8.9 %copy-start.13 = (f32[8]{0:T(128)S(1)}, f32[8]{0:T(128)}, u32[]{:S(2)}) copy-start(f32[8]{0:T(128)} %param.13) | copy-start | bytes 100
  6.5 8.9 %copy-start.9 = (f32[4,4,512]{2,1,0:T(4,128)S(1)}, f32[4,4,512]{2,1,0:T(4,128)}, u32[]{:S(2)}) copy-start(f32[4,4,512]{2,1,0:T(4,128)} %param.12) | copy-start | bytes 98308
  6.5 32.2 %all-to-all-start = ((bf16[130,16,512]{2,0,1:T(8,128)(2,1)}), bf16[130,16,512]{2,0,1:T(8,128)(2,1)}, u32[]{:S(2)}, u32[]{:S(2)}) async-start(bf16[130,16,512]{2,0,1:T(8,128)(2,1)} %pad_maximum_fusion.1), calls=%async_computation | async-start | bytes 4456448 | tf_op jit(solution)/shard_map/all_to_all | solution.py:181
  12.1 28.6 %copy-start.11 = (f32[8]{0:T(128)S(1)}, f32[8]{0:T(128)}, u32[]{:S(2)}) copy-start(f32[8]{0:T(128)} %param.14) | copy-start | bytes 100
  12.1 3.6 %collective-permute-start.1 = (f32[3,4,512]{2,0,1:T(4,128)S(1)}, f32[3,4,512]{2,0,1:T(4,128)S(1)}, u32[]{:S(2)}, u32[]{:S(2)}) collective-permute-start(f32[3,4,512]{2,0,1:T(4,128)S(1)} %get-tuple-element.95), channel_id=1, source_target_pairs={{3,5},{7,9},{11,13},{15,17},{19,21},{23,25},{27,29}} | collective-permute-start | bytes 73736 | tf_op jit(solution)/shard_map/ppermute | solution.py:165
  12.8 2.9 %collective-permute-start.3 = (f32[3,4,512]{2,0,1:T(4,128)S(1)}, f32[3,4,512]{2,0,1:T(4,128)S(1)}, u32[]{:S(2)}, u32[]{:S(2)}) collective-permute-start(f32[3,4,512]{2,0,1:T(4,128)S(1)} %get-tuple-element.96), channel_id=1, source_target_pairs={{3,7},{7,11},{11,15},{15,19},{19,23},{23,27},{27,31}} | collective-permute-start | bytes 73736 | tf_op jit(solution)/shard_map/ppermute | solution.py:165
  13.4 2.2 collective-permute-start.2
  14.1 10.9 %collective-permute-start = (f32[3,4,512]{2,0,1:T(4,128)S(1)}, f32[3,4,512]{2,0,1:T(4,128)S(1)}, u32[]{:S(2)}, u32[]{:S(2)}) collective-permute-start(f32[3,4,512]{2,0,1:T(4,128)S(1)} %get-tuple-element.98), channel_id=1, source_target_pairs={{3,4},{7,8},{11,12},{15,16},{19,20},{23,24},{27,28}} | collective-permute-start | bytes 73736 | tf_op jit(solution)/shard_map/ppermute | solution.py:165
  68.0 2.0 copy-start.1
  70.7 1.0 copy-start.3
  70.7 1.3 copy-start.5
  74.5 4.0 %copy-start.2 = (f32[4,4,2,256,128]{4,3,2,1,0:T(8,128)}, f32[4,4,2,256,128]{4,3,2,1,0:T(8,128)S(1)}, u32[]{:S(2)}) copy-start(f32[4,4,2,256,128]{4,3,2,1,0:T(8,128)S(1)} %broadcast_in_dim.56) | copy-start | bytes 12582916
  85.5 2.1 slice-start
  95.6 2.1 copy-start.7
  113.0 2.3 copy-start.6
  121.1 3.2 %copy-start = (f32[4,8,128,256]{3,2,1,0:T(8,128)}, f32[4,8,128,256]{3,2,1,0:T(8,128)S(1)}, u32[]{:S(2)}) copy-start(f32[4,8,128,256]{3,2,1,0:T(8,128)S(1)} %fusion.15) | copy-start | bytes 12582916
  124.3 50.0 %copy-start.10 = (pred[256]{0:T(512)(128)(4,1)S(1)}, pred[256]{0:T(512)(128)(4,1)}, u32[]{:S(2)}) copy-start(pred[256]{0:T(512)(128)(4,1)} %constant.47.clone.1) | copy-start | bytes 772
  147.3 27.0 %collective-permute-start.4 = (f32[8,128,256]{2,1,0:T(8,128)S(1)}, f32[8,128,256]{2,1,0:T(8,128)S(1)}, u32[]{:S(2)}, u32[]{:S(2)}) collective-permute-start(f32[8,128,256]{2,1,0:T(8,128)S(1)} %get-tuple-element.44), channel_id=1, source_target_pairs={{0,4},{4,8},{8,12},{12,16},{16,20},{20,24},{24,28},{1,5},{5,9},{9,... | collective-permute-start | bytes 3145736 | tf_op jit(solution)/shard_map/ppermute | solution.py:117
  175.4 25.2 %collective-permute-start.5 = (f32[8,128,256]{2,1,0:T(8,128)S(1)}, f32[8,128,256]{2,1,0:T(8,128)S(1)}, u32[]{:S(2)}, u32[]{:S(2)}) collective-permute-start(f32[8,128,256]{2,1,0:T(8,128)S(1)} %fusion.42), channel_id=1, source_target_pairs={{0,8},{4,12},{8,16},{12,20},{16,24},{20,28},{1,9},{5,13},{9,17},{1... | collective-permute-start | bytes 3145736 | tf_op jit(solution)/shard_map/ppermute | solution.py:117
  201.7 13.2 %copy-start.4 = (f32[512,4,128]{2,0,1:T(8,128)S(1)}, f32[512,4,128]{2,0,1:T(8,128)}, u32[]{:S(2)}) copy-start(f32[512,4,128]{2,0,1:T(8,128)} %copy-done.3) | copy-start | bytes 3145732
  201.7 36.5 %collective-permute-start.6 = (f32[8,128,256]{2,1,0:T(8,128)S(1)}, f32[8,128,256]{2,1,0:T(8,128)S(1)}, u32[]{:S(2)}, u32[]{:S(2)}) collective-permute-start(f32[8,128,256]{2,1,0:T(8,128)S(1)} %fusion.41), channel_id=1, source_target_pairs={{0,4},{4,8},{8,12},{12,16},{16,20},{20,24},{24,28},{1,5},{5,9},{9,... | collective-permute-start | bytes 3145736 | tf_op jit(solution)/shard_map/ppermute | solution.py:117
  213.1 2.2 copy-start.8
  213.1 25.0 %collective-permute-start.7 = (f32[8,128,128]{2,1,0:T(8,128)S(1)}, f32[8,128,128]{2,1,0:T(8,128)S(1)}, u32[]{:S(2)}, u32[]{:S(2)}) collective-permute-start(f32[8,128,128]{2,1,0:T(8,128)S(1)} %slice.177), channel_id=1, source_target_pairs={{0,20},{4,24},{8,28},{1,21},{5,25},{9,29},{2,22},{6,26},{10,30},{3... | collective-permute-start | bytes 1572872 | tf_op jit(solution)/shard_map/ppermute | solution.py:117
  238.9 2.8 %copy-start.12 = (f32[128]{0:T(128)S(1)}, f32[128]{0:T(128)}, u32[]{:S(2)}) copy-start(f32[128]{0:T(128)} %param.15) | copy-start | bytes 1540
